TPU v7x, 256 devices: a whole 4x4x8 slice. The times are simulated.
256 devices in a mesh: expert: 16 (over z, core), fsdp: 16 (over x, y).
Axes of the slice: x: 4, y: 4, z: 8, core: 2. Of those that a mesh axis runs over, the one named last changes fastest.
Arguments:
- tokens: bfloat16 [4096, 6144], P(('expert', 'fsdp')), may hold values from -6 to 6
- expert_ids: int32 [4096, 4], P(('expert', 'fsdp')), may hold values from 0 to 15, all different within a row; in each aligned block of 16 rows (0 to 15, 16 to 31, ...) at most 5 rows name the same one
- router_weight: float32 [4096, 4], P(('expert', 'fsdp')), may hold values from 0.1 to 1
- w_gate: bfloat16 [16, 5376, 6144], P('expert', 'fsdp'), may hold values from -0.078125 to 0.078125
- w_up: bfloat16 [16, 5376, 6144], P('expert', 'fsdp'), may hold values from -0.078125 to 0.078125
Outputs:
- routed: bfloat16 [4096, 4, 5376], P(('expert', 'fsdp'))
Inputs may be any that keep to these rules, and one draw needn't show every extreme that they name: `expert_ids`: each row names 4 different experts; the 16 rows of one device name any one expert at most 5 times, and some device names some expert exactly 5 times.
All inputs are finite; a program needn't handle non-finite values.
Results may differ from a plain program's by a relative error of at most 0.0049.
Values may be sent and summed in bfloat16 or wider, within the bound.
No kernel may reach another device: no remote copies, remote signals or barrier semaphores. Data moves between devices by JAX's collectives and lax.ppermute only.
A program may use at most 128 MiB of HBM per device.

v0:
```python
import jax
import jax.numpy as jnp
from jax import lax
from jax.sharding import PartitionSpec as P


def hidden_block(row_block, gate_rows, up_rows):
    gate_act = lax.dot_general(
        row_block, gate_rows, (((1,), (1,)), ((), ())), preferred_element_type=jnp.float32
    )
    up_act = lax.dot_general(
        row_block, up_rows, (((1,), (1,)), ((), ())), preferred_element_type=jnp.float32
    )
    return (jax.nn.gelu(gate_act, approximate=False) * up_act).astype(jnp.bfloat16)


def local(tokens, expert_ids, router_weight, w_gate, w_up):
    tok_rows, model_width = tokens.shape
    top_count = expert_ids.shape[1]
    experts = lax.axis_size("expert")
    fsdp_size = lax.axis_size("fsdp")
    cap_slots = 5 * tok_rows * top_count // (4 * experts)
    flat_ids = expert_ids.reshape(-1)
    choosing = (flat_ids[:, None] == jnp.arange(experts, dtype=jnp.int32)[None, :]).astype(
        jnp.int32
    )
    slot_rank = jnp.sum((jnp.cumsum(choosing, axis=0) - 1) * choosing, axis=1)
    slot_of = flat_ids * cap_slots + slot_rank
    placing = (
        slot_of[None, :] == jnp.arange(experts * cap_slots, dtype=jnp.int32)[:, None]
    ).astype(jnp.bfloat16)
    repeated = jnp.repeat(tokens, top_count, axis=0)
    outgoing = jnp.dot(placing, repeated, preferred_element_type=jnp.float32).astype(jnp.bfloat16)
    outgoing = outgoing.reshape(experts, cap_slots, model_width)
    gate_rows = w_gate[0]
    up_rows = w_up[0]
    columns = gate_rows.shape[0]
    arrived = lax.all_to_all(outgoing, "expert", split_axis=0, concat_axis=0, tiled=True)
    local_hidden = hidden_block(
        lax.all_gather(arrived.reshape(-1, model_width), "fsdp", axis=0, tiled=True),
        gate_rows,
        up_rows,
    )
    shaped = local_hidden.reshape(fsdp_size, experts, cap_slots, columns)
    by_owner = jnp.transpose(shaped, (1, 0, 2, 3)).reshape(experts * fsdp_size, cap_slots, columns)
    returned = lax.all_to_all(by_owner, ("expert", "fsdp"), 0, 0, tiled=True)
    returned = returned.reshape(experts, fsdp_size, cap_slots, columns)
    returned = jnp.transpose(returned, (0, 2, 1, 3)).reshape(experts * cap_slots, -1)
    collected = lax.dot_general(
        placing, returned, (((0,), (0,)), ((), ())), preferred_element_type=jnp.float32
    )
    routed = (router_weight.reshape(-1, 1) * collected).astype(jnp.bfloat16)
    return routed.reshape(tok_rows, top_count, -1)


def solution(mesh):
    return jax.shard_map(
        local,
        mesh=mesh,
        in_specs=(
            P(("expert", "fsdp"), None),
            P(("expert", "fsdp"), None),
            P(("expert", "fsdp"), None),
            P("expert", "fsdp", None),
            P("expert", "fsdp", None),
        ),
        out_specs=P(("expert", "fsdp"), None, None),
        check_vma=False,
    )
```

profile of v0, /device:TPU:8, one launch (start us, length us, event | category | flops | bytes accessed | tf_op | source)
XLA Modules:
  0.0 256.1 jit_solution(8228887948077420177)
XLA Ops:
  6.5 0.0 all-gather.2.cloned.1.call-start
  6.5 0.8 copy.14
  7.3 0.1 reshape.38
  7.4 0.1 fusion.20
  7.5 0.1 reduce_window_sum.11
  7.6 0.2 select_reduce_fusion
  7.8 1.2 broadcast_in_dim.2
  9.0 0.2 reshape.39
  9.2 0.4 convolution_convert_fusion
  9.6 0.5 reshape.40
  10.1 46.9 %all_to_all.10 = bf16[16,5,6144]{2,1,0:T(8,128)(2,1)S(1)} all-to-all(bf16[16,5,6144]{2,1,0:T(8,128)(2,1)S(1)} %reshape.40), channel_id=1, replica_groups=mesh['expert'=16,'fsdp'=16] {'expert'}, dimensions={0} | all-to-all | bytes 1966080 | tf_op jit(solution)/shard_map/all_to_all | solution.py:38
  56.9 1.2 reshape.41
  58.2 0.0 all-gather.2.cloned.1.call-update
  58.2 109.6 %all-gather.2.cloned.1.call-done = bf16[1280,6144]{1,0:T(8,128)(2,1)} async-done(((bf16[80,6144]{1,0:T(8,128)(2,1)}), bf16[1280,6144]{1,0:T(8,128)(2,1)}) %all-gather.2.cloned.1.call-update) | async-done | bytes 15728656 | tf_op jit(solution)/shard_map/all_gather | solution.py:40
  167.8 0.0 copy-start.1
  167.8 0.0 copy-start.2
  167.8 11.7 %fusion.3 = f32[1280,336]{0,1:T(8,128)S(1)} fusion(bf16[1280,6144]{1,0:T(8,128)(2,1)} %all-gather.2.cloned.1.call-done, bf16[1,336,6144]{2,1,0:T(8,128)(2,1)} %param.8), kind=kOutput, calls=%fused_computation.5 | convolution fusion | flops 5284823040 | bytes 21577728 | tf_op jit(solution)/shard_map/dot_general | solution.py:8
  179.6 0.0 copy-done.1
  179.6 0.5 copy-done.2
  180.1 8.9 %fusion.8 = bf16[1280,336]{0,1:T(8,128)(2,1)S(1)} fusion(bf16[1280,6144]{1,0:T(8,128)(2,1)S(1)} %copy-done.1, bf16[1,336,6144]{2,1,0:T(8,128)(2,1)S(1)} %copy-done.2, f32[1280,336]{0,1:T(8,128)S(1)} %fusion.3), kind=kOutput, calls=%fused_computation.8 | convolution fusion | flops 5313208320 | bytes 22437888 | tf_op jit(solution)/shard_map/dot_general | solution.py:11
  189.0 0.6 copy.15
  189.7 0.7 reshape.42
  190.3 0.7 copy.16
  191.0 1.8 copy.17
  192.8 0.0 copy-start
  192.8 11.5 %all-to-all-start.1 = ((bf16[256,5,336]{2,1,0:T(8,128)(2,1)}), bf16[256,5,336]{2,1,0:T(8,128)(2,1)S(1)}, u32[]{:S(2)}, u32[]{:S(2)}) async-start(bf16[256,5,336]{2,1,0:T(8,128)(2,1)} %copy.17), calls=%async_computation.1 | async-start | bytes 3145728 | tf_op jit(solution)/shard_map/all_to_all | solution.py:46
  204.4 0.0 copy-done
  204.4 0.1 copy.13
  204.5 0.1 mul.41
  204.6 42.0 %all-to-all-done.1 = bf16[256,5,336]{2,1,0:T(8,128)(2,1)S(1)} async-done(((bf16[256,5,336]{2,1,0:T(8,128)(2,1)}), bf16[256,5,336]{2,1,0:T(8,128)(2,1)S(1)}, u32[]{:S(2)}, u32[]{:S(2)}) %all-to-all-start.1) | async-done | bytes 860192 | tf_op jit(solution)/shard_map/all_to_all | solution.py:46
  246.5 0.1 copy.20
  246.7 1.2 reshape.45
  247.9 0.4 fusion
  248.3 1.0 reshape.46
  (1 shorter events, 0.0 us)
Async XLA Ops:
  6.5 161.3 %all-gather.2.cloned.1.call-start = ((), (), s32[]{:S(2)}) async-start(), calls=%async_computation.2 | async-start | bytes 16711680 | tf_op jit(solution)/shard_map/all_gather | solution.py:40
  167.8 11.8 %copy-start.1 = (bf16[1280,6144]{1,0:T(8,128)(2,1)S(1)}, bf16[1280,6144]{1,0:T(8,128)(2,1)}, u32[]{:S(2)}) copy-start(bf16[1280,6144]{1,0:T(8,128)(2,1)} %all-gather.2.cloned.1.call-done) | copy-start | bytes 47185924
  167.8 12.3 %copy-start.2 = (bf16[1,336,6144]{2,1,0:T(8,128)(2,1)S(1)}, bf16[1,336,6144]{2,1,0:T(8,128)(2,1)}, u32[]{:S(2)}) copy-start(bf16[1,336,6144]{2,1,0:T(8,128)(2,1)} %param.9) | copy-start | bytes 12386308
  192.8 11.5 %copy-start = (f32[16,4]{0,1:T(4,128)S(1)}, f32[16,4]{0,1:T(4,128)}, u32[]{:S(2)}) copy-start(f32[16,4]{0,1:T(4,128)} %param.7) | copy-start | bytes 772
  192.8 53.7 %all-to-all-start.1 = ((bf16[256,5,336]{2,1,0:T(8,128)(2,1)}), bf16[256,5,336]{2,1,0:T(8,128)(2,1)S(1)}, u32[]{:S(2)}, u32[]{:S(2)}) async-start(bf16[256,5,336]{2,1,0:T(8,128)(2,1)} %copy.17), calls=%async_computation.1 | async-start | bytes 3145728 | tf_op jit(solution)/shard_map/all_to_all | solution.py:46
Sparse Core Ops, SparseCore 0:
  58.3 109.4 all-gather.1
where the time goes:
time: 256 us
  waiting for transfers between devices  152 us (59%)
  blocking collectives  46.9 us (18%)
  matrix products  21.5 us (8%)
  between operations  13.5 us (5%)
  starting transfers between devices  11.5 us (4%)
  local copies, waits for them, and re-layouts  10.8 us (4%)
    all_gather x1, waiting for transfers between devices, local(): lax.all_gather(arrived.reshape(-1, model_width), 'fsdp', axis=0, tiled=True)  110 us
    all_to_all x1, blocking collectives, local(): lax.all_to_all(outgoing, 'expert', split_axis=0, concat_axis=0, tiled=True)  46.9 us
    all_to_all x1, waiting for transfers between devices, local(): returned = lax.all_to_all(by_owner, ('expert', 'fsdp'), 0, 0, tiled=True)  42 us
    dot_general x1, matrix products, hidden_block(): lax.dot_general(row_block, gate_rows, (((1,), (1,)), ((), ())), preferred...  11.7 us
    all_to_all x1, starting transfers between devices, local(): returned = lax.all_to_all(by_owner, ('expert', 'fsdp'), 0, 0, tiled=True)  11.5 us
    dot_general x1, matrix products, hidden_block(): lax.dot_general(row_block, up_rows, (((1,), (1,)), ((), ())), preferred_e...  8.94 us
  transfers between devices with their start and end apart: 2, of which 2 were waited for; matrix products, arithmetic and copies ran while one was open for 0% of the time, Pallas kernels for 0%

commit v1 on v0

--- a/solution.py
+++ b/solution.py
@@ -2,6 +2,24 @@
 import jax.numpy as jnp
 from jax import lax
 from jax.sharding import PartitionSpec as P
+
+
+def ring_gather(value, axis, dim):
+    ways, here, step = (lax.axis_size(axis), lax.axis_index(axis), value.shape[dim])
+    lengths = [n * ways if d == dim else n for d, n in enumerate(value.shape)]
+    full = lax.dynamic_update_slice_in_dim(
+        jnp.zeros(lengths, value.dtype), value, here * step, axis=dim
+    )
+    going_up = going_down = value
+    for far in range(1, ways // 2 + 1):
+        going_up = lax.ppermute(going_up, axis, [(d, (d + 1) % ways) for d in range(ways)])
+        full = lax.dynamic_update_slice_in_dim(full, going_up, (here - far) % ways * step, axis=dim)
+        if 2 * far < ways:
+            going_down = lax.ppermute(going_down, axis, [(d, (d - 1) % ways) for d in range(ways)])
+            full = lax.dynamic_update_slice_in_dim(
+                full, going_down, (here + far) % ways * step, axis=dim
+            )
+    return full
 
 
 def hidden_block(row_block, gate_rows, up_rows):
@@ -37,9 +55,7 @@
     columns = gate_rows.shape[0]
     arrived = lax.all_to_all(outgoing, "expert", split_axis=0, concat_axis=0, tiled=True)
     local_hidden = hidden_block(
-        lax.all_gather(arrived.reshape(-1, model_width), "fsdp", axis=0, tiled=True),
-        gate_rows,
-        up_rows,
+        ring_gather(arrived.reshape(-1, model_width), "fsdp", 0), gate_rows, up_rows
     )
     shaped = local_hidden.reshape(fsdp_size, experts, cap_slots, columns)
     by_owner = jnp.transpose(shaped, (1, 0, 2, 3)).reshape(experts * fsdp_size, cap_slots, columns)

time: 256 us -> 334 us (1.30)
  waiting for transfers between devices: 152 us -> 186 us
  starting transfers between devices: 11.5 us -> 41.1 us
  local copies, waits for them, and re-layouts: 10.8 us -> 34.1 us
  between operations: 13.5 us -> 0.16 us
  matrix products: 21.5 us -> 25.3 us
    ppermute x0 -> x15, waiting for transfers between devices: none -> 144 us  [the longest x8 143 us: ring_gather(): lax.ppermute(going_up, axis, [(d, (d + 1) % ways) for d in range(ways)])]
    all_gather x1 -> x0, waiting for transfers between devices: 110 us -> none  [local(): lax.all_gather(arrived.reshape(-1, model_width), 'fsdp', axis=0, tiled=True)]
    ppermute x0 -> x15, starting transfers between devices: none -> 30.7 us  [the longest x7 27.5 us: ring_gather(): lax.ppermute(going_down, axis, [(d, (d - 1) % ways) for d in range(ways)])]
    dynamic_update_slice x0 -> x16, local copies, waits for them, and re-layouts: none -> 16.6 us  [the longest x8 8.24 us: ring_gather(): lax.dynamic_update_slice_in_dim(full, going_up, (here - far) % ways * ste...]
    broadcast_in_dim x0 -> x1, local copies, waits for them, and re-layouts: none -> 7.48 us  [ring_gather(): jnp.zeros(lengths, value.dtype)]
    dot_general x1, matrix products: 8.94 us -> 15.3 us  [hidden_block(): lax.dot_general(row_block, up_rows, (((1,), (1,)), ((), ())), preferred_e...]
  transfers between devices with their start and end apart: 2 -> 16, of which waited for: 2 -> 10; matrix products, arithmetic and copies ran while one was open for 0% -> 7% of each run, Pallas kernels for 0% -> 0%
where the time goes in v1:
time: 334 us
  waiting for transfers between devices  186 us (56%)
  blocking collectives  46.9 us (14%)
  starting transfers between devices  41.1 us (12%)
  local copies, waits for them, and re-layouts  34.1 us (10%)
  matrix products  25.3 us (8%)
    ppermute x8, waiting for transfers between devices, ring_gather(): lax.ppermute(going_up, axis, [(d, (d + 1) % ways) for d in range(ways)])  143 us
    all_to_all x1, blocking collectives, local(): lax.all_to_all(outgoing, 'expert', split_axis=0, concat_axis=0, tiled=True)  46.9 us
    all_to_all x1, waiting for transfers between devices, local(): returned = lax.all_to_all(by_owner, ('expert', 'fsdp'), 0, 0, tiled=True)  42.1 us
    ppermute x7, starting transfers between devices, ring_gather(): lax.ppermute(going_down, axis, [(d, (d - 1) % ways) for d in range(ways)])  27.5 us
    dot_general x1, matrix products, hidden_block(): lax.dot_general(row_block, up_rows, (((1,), (1,)), ((), ())), preferred_e...  15.3 us
    all_to_all x1, starting transfers between devices, local(): returned = lax.all_to_all(by_owner, ('expert', 'fsdp'), 0, 0, tiled=True)  10.3 us
    dot_general x1, matrix products, hidden_block(): lax.dot_general(row_block, gate_rows, (((1,), (1,)), ((), ())), preferred...  9.16 us
    dynamic_update_slice x8, local copies, waits for them, and re-layouts, ring_gather(): lax.dynamic_update_slice_in_dim(full, going_up, (here - far) % ways * ste...  8.24 us
  transfers between devices with their start and end apart: 16, of which 10 were waited for; matrix products, arithmetic and copies ran while one was open for 7% of the time, Pallas kernels for 0%

profile of v1, /device:TPU:8, one launch (start us, length us, event | category | flops | bytes accessed | tf_op | source)
XLA Modules:
  0.0 333.7 jit_solution(9685278580501751007)
XLA Ops:
  0.0 0.8 copy.14
  0.8 0.1 reshape.38
  0.8 0.1 fusion.16
  0.9 0.1 reduce_window_sum.11
  1.0 0.2 select_reduce_fusion
  1.2 1.2 broadcast_in_dim.10
  2.5 0.2 reshape.39
  2.6 0.4 convolution_convert_fusion
  3.0 0.5 reshape.40
  3.5 46.9 %all_to_all.10 = bf16[16,5,6144]{2,1,0:T(8,128)(2,1)S(1)} all-to-all(bf16[16,5,6144]{2,1,0:T(8,128)(2,1)S(1)} %reshape.40), channel_id=1, replica_groups=mesh['expert'=16,'fsdp'=16] {'expert'}, dimensions={0} | all-to-all | bytes 1966080 | tf_op jit(solution)/shard_map/all_to_all | solution.py:56
  50.4 0.5 reshape.41
  50.9 1.7 collective-permute-start
  52.5 0.4 collective-permute-start.1
  53.0 7.5 %broadcast_in_dim.4 = bf16[1280,6144]{1,0:T(8,128)(2,1)} broadcast(bf16[]{:T(256)} %constant.129.clone.1), dimensions={} | broadcast | bytes 15728642 | tf_op jit(solution)/shard_map/broadcast_in_dim | solution.py:11
  60.5 1.1 constant_dynamic-update-slice_fusion.14
  61.6 13.3 %collective-permute-done = bf16[80,6144]{1,0:T(8,128)(2,1)S(1)} collective-permute-done((bf16[80,6144]{1,0:T(8,128)(2,1)S(1)}, bf16[80,6144]{1,0:T(8,128)(2,1)S(1)}, u32[]{:S(2)}, u32[]{:S(2)}) %collective-permute-start) | collective-permute-done | bytes 983072 | tf_op jit(solution)/shard_map/ppermute | solution.py:15
  74.9 1.6 collective-permute-start.2
  76.5 0.3 collective-permute-done.1
  76.8 1.7 collective-permute-start.3
  78.5 1.0 constant_dynamic-update-slice_fusion.13
  79.5 1.0 constant_dynamic-update-slice_fusion.12
  80.6 20.5 %collective-permute-done.2 = bf16[80,6144]{1,0:T(8,128)(2,1)S(1)} collective-permute-done((bf16[80,6144]{1,0:T(8,128)(2,1)S(1)}, bf16[80,6144]{1,0:T(8,128)(2,1)S(1)}, u32[]{:S(2)}, u32[]{:S(2)}) %collective-permute-start.2) | collective-permute-done | bytes 983072 | tf_op jit(solution)/shard_map/ppermute | solution.py:15
  101.1 0.0 collective-permute-done.3
  101.1 5.1 %collective-permute-start.5 = (bf16[80,6144]{1,0:T(8,128)(2,1)S(1)}, bf16[80,6144]{1,0:T(8,128)(2,1)S(1)}, u32[]{:S(2)}, u32[]{:S(2)}) collective-permute-start(bf16[80,6144]{1,0:T(8,128)(2,1)S(1)} %collective-permute-done.3), channel_id=1, source_target_pairs={{0,15},{1,0},{2,1},{3,2},{4,3},{5,4},{6,5},{7,6},{8,7},{9,8},{10,9... | collective-permute-start | bytes 2949128 | tf_op jit(solution)/shard_map/ppermute | solution.py:18
  106.2 1.0 constant_dynamic-update-slice_fusion.11
  107.2 1.0 constant_dynamic-update-slice_fusion.10
  108.2 19.7 %collective-permute-done.4 = bf16[80,6144]{1,0:T(8,128)(2,1)S(1)} collective-permute-done((bf16[80,6144]{1,0:T(8,128)(2,1)S(1)}, bf16[80,6144]{1,0:T(8,128)(2,1)S(1)}, u32[]{:S(2)}, u32[]{:S(2)}) %collective-permute-start.4) | collective-permute-done | bytes 983072 | tf_op jit(solution)/shard_map/ppermute | solution.py:15
  127.9 0.0 collective-permute-start.6
  127.9 0.0 collective-permute-done.5
  127.9 5.1 %collective-permute-start.7 = (bf16[80,6144]{1,0:T(8,128)(2,1)S(1)}, bf16[80,6144]{1,0:T(8,128)(2,1)S(1)}, u32[]{:S(2)}, u32[]{:S(2)}) collective-permute-start(bf16[80,6144]{1,0:T(8,128)(2,1)S(1)} %collective-permute-done.5), channel_id=1, source_target_pairs={{0,15},{1,0},{2,1},{3,2},{4,3},{5,4},{6,5},{7,6},{8,7},{9,8},{10,9... | collective-permute-start | bytes 2949128 | tf_op jit(solution)/shard_map/ppermute | solution.py:18
  133.0 1.0 constant_dynamic-update-slice_fusion.9
  134.0 1.0 constant_dynamic-update-slice_fusion.8
  135.0 18.9 %collective-permute-done.6 = bf16[80,6144]{1,0:T(8,128)(2,1)S(1)} collective-permute-done((bf16[80,6144]{1,0:T(8,128)(2,1)S(1)}, bf16[80,6144]{1,0:T(8,128)(2,1)S(1)}, u32[]{:S(2)}, u32[]{:S(2)}) %collective-permute-start.6) | collective-permute-done | bytes 983072 | tf_op jit(solution)/shard_map/ppermute | solution.py:15
  153.9 5.1 %collective-permute-start.9 = (bf16[80,6144]{1,0:T(8,128)(2,1)S(1)}, bf16[80,6144]{1,0:T(8,128)(2,1)S(1)}, u32[]{:S(2)}, u32[]{:S(2)}) collective-permute-start(bf16[80,6144]{1,0:T(8,128)(2,1)S(1)} %collective-permute-done.7), channel_id=1, source_target_pairs={{0,15},{1,0},{2,1},{3,2},{4,3},{5,4},{6,5},{7,6},{8,7},{9,8},{10,9... | collective-permute-start | bytes 2949128 | tf_op jit(solution)/shard_map/ppermute | solution.py:18
  158.9 1.1 constant_dynamic-update-slice_fusion.7
  160.0 1.0 constant_dynamic-update-slice_fusion.6
  161.0 17.8 %collective-permute-done.8 = bf16[80,6144]{1,0:T(8,128)(2,1)S(1)} collective-permute-done((bf16[80,6144]{1,0:T(8,128)(2,1)S(1)}, bf16[80,6144]{1,0:T(8,128)(2,1)S(1)}, u32[]{:S(2)}, u32[]{:S(2)}) %collective-permute-start.8) | collective-permute-done | bytes 983072 | tf_op jit(solution)/shard_map/ppermute | solution.py:15
  178.9 5.1 %collective-permute-start.11 = (bf16[80,6144]{1,0:T(8,128)(2,1)S(1)}, bf16[80,6144]{1,0:T(8,128)(2,1)S(1)}, u32[]{:S(2)}, u32[]{:S(2)}) collective-permute-start(bf16[80,6144]{1,0:T(8,128)(2,1)S(1)} %collective-permute-done.9), channel_id=1, source_target_pairs={{0,15},{1,0},{2,1},{3,2},{4,3},{5,4},{6,5},{7,6},{8,7},{9,8},{10,9... | collective-permute-start | bytes 2949128 | tf_op jit(solution)/shard_map/ppermute | solution.py:18
  183.9 1.0 constant_dynamic-update-slice_fusion.5
  185.0 1.0 constant_dynamic-update-slice_fusion.4
  186.0 17.0 %collective-permute-done.10 = bf16[80,6144]{1,0:T(8,128)(2,1)S(1)} collective-permute-done((bf16[80,6144]{1,0:T(8,128)(2,1)S(1)}, bf16[80,6144]{1,0:T(8,128)(2,1)S(1)}, u32[]{:S(2)}, u32[]{:S(2)}) %collective-permute-start.10) | collective-permute-done | bytes 983072 | tf_op jit(solution)/shard_map/ppermute | solution.py:15
  203.0 5.1 %collective-permute-start.13 = (bf16[80,6144]{1,0:T(8,128)(2,1)S(1)}, bf16[80,6144]{1,0:T(8,128)(2,1)S(1)}, u32[]{:S(2)}, u32[]{:S(2)}) collective-permute-start(bf16[80,6144]{1,0:T(8,128)(2,1)S(1)} %collective-permute-done.11), channel_id=1, source_target_pairs={{0,15},{1,0},{2,1},{3,2},{4,3},{5,4},{6,5},{7,6},{8,7},{9,8},{10,9... | collective-permute-start | bytes 2949128 | tf_op jit(solution)/shard_map/ppermute | solution.py:18
  208.0 1.0 constant_dynamic-update-slice_fusion.3
  209.1 1.0 constant_dynamic-update-slice_fusion.2
  210.1 16.1 %collective-permute-done.12 = bf16[80,6144]{1,0:T(8,128)(2,1)S(1)} collective-permute-done((bf16[80,6144]{1,0:T(8,128)(2,1)S(1)}, bf16[80,6144]{1,0:T(8,128)(2,1)S(1)}, u32[]{:S(2)}, u32[]{:S(2)}) %collective-permute-start.12) | collective-permute-done | bytes 983072 | tf_op jit(solution)/shard_map/ppermute | solution.py:15
  226.2 1.0 constant_dynamic-update-slice_fusion.1
  227.2 1.1 constant_dynamic-update-slice_fusion
  228.3 20.1 %collective-permute-done.14 = bf16[80,6144]{1,0:T(8,128)(2,1)S(1)} collective-permute-done((bf16[80,6144]{1,0:T(8,128)(2,1)S(1)}, bf16[80,6144]{1,0:T(8,128)(2,1)S(1)}, u32[]{:S(2)}, u32[]{:S(2)}) %collective-permute-start.14) | collective-permute-done | bytes 983072 | tf_op jit(solution)/shard_map/ppermute | solution.py:15
  248.4 1.0 constant_dynamic-update-slice_fusion.15
  249.5 9.2 %fusion.3 = f32[1280,336]{0,1:T(8,128)S(1)} fusion(bf16[1280,6144]{1,0:T(8,128)(2,1)} %constant_dynamic-update-slice_fusion.15, bf16[1,336,6144]{2,1,0:T(8,128)(2,1)S(1)} %copy-done.2), kind=kOutput, calls=%fused_computation.5 | convolution fusion | flops 5284823040 | bytes 21577728 | tf_op jit(solution)/shard_map/dot_general | solution.py:26
  258.6 0.8 copy-done
  259.4 15.3 %fusion.8 = bf16[1280,336]{0,1:T(8,128)(2,1)S(1)} fusion(f32[1280,336]{0,1:T(8,128)S(1)} %fusion.3, bf16[1280,6144]{1,0:T(8,128)(2,1)S(1)} %copy-done, bf16[1,336,6144]{2,1,0:T(8,128)(2,1)} %param.9), kind=kOutput, calls=%fused_computation.11 | convolution fusion | flops 5313208320 | bytes 22437888 | tf_op jit(solution)/shard_map/dot_general | solution.py:29
  274.7 0.6 copy.15
  275.4 0.5 reshape.42
  275.9 0.7 copy.16
  276.6 1.8 copy.17
  278.4 10.3 %all-to-all-start.1 = ((bf16[256,5,336]{2,1,0:T(8,128)(2,1)}), bf16[256,5,336]{2,1,0:T(8,128)(2,1)S(1)}, u32[]{:S(2)}, u32[]{:S(2)}) async-start(bf16[256,5,336]{2,1,0:T(8,128)(2,1)} %copy.17), calls=%async_computation.1 | async-start | bytes 3145728 | tf_op jit(solution)/shard_map/all_to_all | solution.py:62
  288.7 0.1 copy.13
  288.8 0.1 mul.89
  288.9 42.1 %all-to-all-done.1 = bf16[256,5,336]{2,1,0:T(8,128)(2,1)S(1)} async-done(((bf16[256,5,336]{2,1,0:T(8,128)(2,1)}), bf16[256,5,336]{2,1,0:T(8,128)(2,1)S(1)}, u32[]{:S(2)}, u32[]{:S(2)}) %all-to-all-start.1) | async-done | bytes 860192 | tf_op jit(solution)/shard_map/all_to_all | solution.py:62
  331.0 0.1 copy.20
  331.1 1.2 reshape.45
  332.3 0.4 fusion
  332.7 1.0 reshape.46
  (15 shorter events, 0.0 us)
Async XLA Ops:
  50.9 24.0 %collective-permute-start = (bf16[80,6144]{1,0:T(8,128)(2,1)S(1)}, bf16[80,6144]{1,0:T(8,128)(2,1)S(1)}, u32[]{:S(2)}, u32[]{:S(2)}) collective-permute-start(bf16[80,6144]{1,0:T(8,128)(2,1)S(1)} %reshape.41), channel_id=1, source_target_pairs={{0,1},{1,2},{2,3},{3,4},{4,5},{5,6},{6,7},{7,8},{8,9},{9,10},{10,1... | collective-permute-start | bytes 2949128 | tf_op jit(solution)/shard_map/ppermute | solution.py:15
  52.5 24.3 %collective-permute-start.1 = (bf16[80,6144]{1,0:T(8,128)(2,1)S(1)}, bf16[80,6144]{1,0:T(8,128)(2,1)S(1)}, u32[]{:S(2)}, u32[]{:S(2)}) collective-permute-start(bf16[80,6144]{1,0:T(8,128)(2,1)S(1)} %reshape.41), channel_id=1, source_target_pairs={{0,15},{1,0},{2,1},{3,2},{4,3},{5,4},{6,5},{7,6},{8,7},{9,8},{10,9... | collective-permute-start | bytes 2949128 | tf_op jit(solution)/shard_map/ppermute | solution.py:18
  74.9 26.2 %collective-permute-start.2 = (bf16[80,6144]{1,0:T(8,128)(2,1)S(1)}, bf16[80,6144]{1,0:T(8,128)(2,1)S(1)}, u32[]{:S(2)}, u32[]{:S(2)}) collective-permute-start(bf16[80,6144]{1,0:T(8,128)(2,1)S(1)} %collective-permute-done), channel_id=1, source_target_pairs={{0,1},{1,2},{2,3},{3,4},{4,5},{5,6},{6,7},{7,8},{8,9},{9,10},{10,1... | collective-permute-start | bytes 2949128 | tf_op jit(solution)/shard_map/ppermute | solution.py:15
  76.8 24.3 %collective-permute-start.3 = (bf16[80,6144]{1,0:T(8,128)(2,1)S(1)}, bf16[80,6144]{1,0:T(8,128)(2,1)S(1)}, u32[]{:S(2)}, u32[]{:S(2)}) collective-permute-start(bf16[80,6144]{1,0:T(8,128)(2,1)S(1)} %collective-permute-done.1), channel_id=1, source_target_pairs={{0,15},{1,0},{2,1},{3,2},{4,3},{5,4},{6,5},{7,6},{8,7},{9,8},{10,9... | collective-permute-start | bytes 2949128 | tf_op jit(solution)/shard_map/ppermute | solution.py:18
  101.1 26.8 %collective-permute-start.4 = (bf16[80,6144]{1,0:T(8,128)(2,1)S(1)}, bf16[80,6144]{1,0:T(8,128)(2,1)S(1)}, u32[]{:S(2)}, u32[]{:S(2)}) collective-permute-start(bf16[80,6144]{1,0:T(8,128)(2,1)S(1)} %collective-permute-done.2), channel_id=1, source_target_pairs={{0,1},{1,2},{2,3},{3,4},{4,5},{5,6},{6,7},{7,8},{8,9},{9,10},{10,1... | collective-permute-start | bytes 2949128 | tf_op jit(solution)/shard_map/ppermute | solution.py:15
  101.1 26.8 %collective-permute-start.5 = (bf16[80,6144]{1,0:T(8,128)(2,1)S(1)}, bf16[80,6144]{1,0:T(8,128)(2,1)S(1)}, u32[]{:S(2)}, u32[]{:S(2)}) collective-permute-start(bf16[80,6144]{1,0:T(8,128)(2,1)S(1)} %collective-permute-done.3), channel_id=1, source_target_pairs={{0,15},{1,0},{2,1},{3,2},{4,3},{5,4},{6,5},{7,6},{8,7},{9,8},{10,9... | collective-permute-start | bytes 2949128 | tf_op jit(solution)/shard_map/ppermute | solution.py:18
  127.9 25.9 %collective-permute-start.6 = (bf16[80,6144]{1,0:T(8,128)(2,1)S(1)}, bf16[80,6144]{1,0:T(8,128)(2,1)S(1)}, u32[]{:S(2)}, u32[]{:S(2)}) collective-permute-start(bf16[80,6144]{1,0:T(8,128)(2,1)S(1)} %collective-permute-done.4), channel_id=1, source_target_pairs={{0,1},{1,2},{2,3},{3,4},{4,5},{5,6},{6,7},{7,8},{8,9},{9,10},{10,1... | collective-permute-start | bytes 2949128 | tf_op jit(solution)/shard_map/ppermute | solution.py:15
  127.9 25.9 %collective-permute-start.7 = (bf16[80,6144]{1,0:T(8,128)(2,1)S(1)}, bf16[80,6144]{1,0:T(8,128)(2,1)S(1)}, u32[]{:S(2)}, u32[]{:S(2)}) collective-permute-start(bf16[80,6144]{1,0:T(8,128)(2,1)S(1)} %collective-permute-done.5), channel_id=1, source_target_pairs={{0,15},{1,0},{2,1},{3,2},{4,3},{5,4},{6,5},{7,6},{8,7},{9,8},{10,9... | collective-permute-start | bytes 2949128 | tf_op jit(solution)/shard_map/ppermute | solution.py:18
  153.9 25.0 %collective-permute-start.8 = (bf16[80,6144]{1,0:T(8,128)(2,1)S(1)}, bf16[80,6144]{1,0:T(8,128)(2,1)S(1)}, u32[]{:S(2)}, u32[]{:S(2)}) collective-permute-start(bf16[80,6144]{1,0:T(8,128)(2,1)S(1)} %collective-permute-done.6), channel_id=1, source_target_pairs={{0,1},{1,2},{2,3},{3,4},{4,5},{5,6},{6,7},{7,8},{8,9},{9,10},{10,1... | collective-permute-start | bytes 2949128 | tf_op jit(solution)/shard_map/ppermute | solution.py:15
  153.9 25.0 %collective-permute-start.9 = (bf16[80,6144]{1,0:T(8,128)(2,1)S(1)}, bf16[80,6144]{1,0:T(8,128)(2,1)S(1)}, u32[]{:S(2)}, u32[]{:S(2)}) collective-permute-start(bf16[80,6144]{1,0:T(8,128)(2,1)S(1)} %collective-permute-done.7), channel_id=1, source_target_pairs={{0,15},{1,0},{2,1},{3,2},{4,3},{5,4},{6,5},{7,6},{8,7},{9,8},{10,9... | collective-permute-start | bytes 2949128 | tf_op jit(solution)/shard_map/ppermute | solution.py:18
  178.9 24.1 %collective-permute-start.10 = (bf16[80,6144]{1,0:T(8,128)(2,1)S(1)}, bf16[80,6144]{1,0:T(8,128)(2,1)S(1)}, u32[]{:S(2)}, u32[]{:S(2)}) collective-permute-start(bf16[80,6144]{1,0:T(8,128)(2,1)S(1)} %collective-permute-done.8), channel_id=1, source_target_pairs={{0,1},{1,2},{2,3},{3,4},{4,5},{5,6},{6,7},{7,8},{8,9},{9,10},{10,1... | collective-permute-start | bytes 2949128 | tf_op jit(solution)/shard_map/ppermute | solution.py:15
  178.9 24.1 %collective-permute-start.11 = (bf16[80,6144]{1,0:T(8,128)(2,1)S(1)}, bf16[80,6144]{1,0:T(8,128)(2,1)S(1)}, u32[]{:S(2)}, u32[]{:S(2)}) collective-permute-start(bf16[80,6144]{1,0:T(8,128)(2,1)S(1)} %collective-permute-done.9), channel_id=1, source_target_pairs={{0,15},{1,0},{2,1},{3,2},{4,3},{5,4},{6,5},{7,6},{8,7},{9,8},{10,9... | collective-permute-start | bytes 2949128 | tf_op jit(solution)/shard_map/ppermute | solution.py:18
  203.0 23.2 %collective-permute-start.12 = (bf16[80,6144]{1,0:T(8,128)(2,1)S(1)}, bf16[80,6144]{1,0:T(8,128)(2,1)S(1)}, u32[]{:S(2)}, u32[]{:S(2)}) collective-permute-start(bf16[80,6144]{1,0:T(8,128)(2,1)S(1)} %collective-permute-done.10), channel_id=1, source_target_pairs={{0,1},{1,2},{2,3},{3,4},{4,5},{5,6},{6,7},{7,8},{8,9},{9,10},{10,1... | collective-permute-start | bytes 2949128 | tf_op jit(solution)/shard_map/ppermute | solution.py:15
  203.0 24.2 %collective-permute-start.13 = (bf16[80,6144]{1,0:T(8,128)(2,1)S(1)}, bf16[80,6144]{1,0:T(8,128)(2,1)S(1)}, u32[]{:S(2)}, u32[]{:S(2)}) collective-permute-start(bf16[80,6144]{1,0:T(8,128)(2,1)S(1)} %collective-permute-done.11), channel_id=1, source_target_pairs={{0,15},{1,0},{2,1},{3,2},{4,3},{5,4},{6,5},{7,6},{8,7},{9,8},{10,9... | collective-permute-start | bytes 2949128 | tf_op jit(solution)/shard_map/ppermute | solution.py:18
  226.2 22.3 %collective-permute-start.14 = (bf16[80,6144]{1,0:T(8,128)(2,1)S(1)}, bf16[80,6144]{1,0:T(8,128)(2,1)S(1)}, u32[]{:S(2)}, u32[]{:S(2)}) collective-permute-start(bf16[80,6144]{1,0:T(8,128)(2,1)S(1)} %collective-permute-done.12), channel_id=1, source_target_pairs={{0,1},{1,2},{2,3},{3,4},{4,5},{5,6},{6,7},{7,8},{8,9},{9,10},{10,1... | collective-permute-start | bytes 2949128 | tf_op jit(solution)/shard_map/ppermute | solution.py:15
  226.2 23.3 %copy-start.2 = (bf16[1,336,6144]{2,1,0:T(8,128)(2,1)S(1)}, bf16[1,336,6144]{2,1,0:T(8,128)(2,1)}, u32[]{:S(2)}) copy-start(bf16[1,336,6144]{2,1,0:T(8,128)(2,1)} %param.8) | copy-start | bytes 12386308
  249.5 9.9 %copy-start = (bf16[1280,6144]{1,0:T(8,128)(2,1)S(1)}, bf16[1280,6144]{1,0:T(8,128)(2,1)}, u32[]{:S(2)}) copy-start(bf16[1280,6144]{1,0:T(8,128)(2,1)} %constant_dynamic-update-slice_fusion.15) | copy-start | bytes 47185924
  278.4 10.4 %copy-start.1 = (f32[16,4]{0,1:T(4,128)S(1)}, f32[16,4]{0,1:T(4,128)}, u32[]{:S(2)}) copy-start(f32[16,4]{0,1:T(4,128)} %param.7) | copy-start | bytes 772
  278.4 52.6 %all-to-all-start.1 = ((bf16[256,5,336]{2,1,0:T(8,128)(2,1)}), bf16[256,5,336]{2,1,0:T(8,128)(2,1)S(1)}, u32[]{:S(2)}, u32[]{:S(2)}) async-start(bf16[256,5,336]{2,1,0:T(8,128)(2,1)} %copy.17), calls=%async_computation.1 | async-start | bytes 3145728 | tf_op jit(solution)/shard_map/all_to_all | solution.py:62
